TPU v7x, 32 devices: a whole 2x2x4 slice. The times are simulated.
32 devices in a mesh: groups: 1, orb: 32 (over z, y, x, core), aux: 1.
Axes of the slice: x: 2, y: 2, z: 4, core: 2. Of those that a mesh axis runs over, the one named last changes fastest.
Arguments:
- exchange_integral_halves: float32 [1, 128, 256, 256], P('aux', ('groups', 'orb')), may hold values from -3 to 3
- amplitudes: bfloat16 [128, 256, 256], P(('groups', 'orb')), may hold values from -6 to 6
- pair_slot_orbitals: int32 [128, 2], P('groups'), may hold values from 0 to 63
- pao_domain: int32 [64, 256], P('groups'), may hold values from 0 to 511, as said below
- pao_intersection: bfloat16 [512, 512], P('groups'), as said below
- pao_fock: bfloat16 [512, 512], P('groups'), as said below
- occ_energy: float32 [64], P('groups'), may hold values from -1.5 to -0.3
- coupled_pair_owner: int32 [128, 8], P(('groups', 'orb')), may hold values from 0 to 31, all different within a row; in each aligned block of 4 rows (0 to 3, 4 to 7, ...) at most 2 rows name the same one
- coupled_pair_slot: int32 [128, 8], P(('groups', 'orb')), may hold values from 0 to 3
- coupling_swap_flag: int32 [128, 8], P(('groups', 'orb')), may hold values from 0 to 1
- coupling_fock_element: float32 [128, 8], P(('groups', 'orb')), may hold values from -1.2 to 1.2
Outputs:
- residual: float32 [128, 256, 256], P(('groups', 'orb'), 'aux')
- updated_pair_amplitudes: bfloat16 [128, 256, 256], P(('groups', 'orb'), 'aux')
Inputs may be any that keep to these rules, and one draw needn't show every extreme that they name: `pao_domain`: each orbital's 256 domain entries are distinct. `coupled_pair_owner`: the 8 owners in one row differ; among the 4 pair slots of one owner no owner is named by more than 2 rows, a bound that some block reaches. `pao_intersection`: symmetric with unit diagonal. `pao_fock`: symmetric with diagonal from 0.5 to 3.
All inputs are finite; a program needn't handle non-finite values.
Results may differ from a plain program's by a relative error of at most 0.012.
Values may be sent and summed in bfloat16 or wider, within the bound.
No kernel may reach another device: no remote copies, remote signals or barrier semaphores. Data moves between devices by JAX's collectives and lax.ppermute only.
A program may use at most 128 MiB of HBM per device.

v0:
```python
import jax
import jax.numpy as jnp
from jax import lax
from jax.sharding import PartitionSpec as P


def one_hot(ids, width):
    return (ids[..., None] == jnp.arange(width, dtype=ids.dtype)).astype(jnp.bfloat16)


def sel_rows(onehot, matrix):
    return jnp.einsum("...rk,kc->...rc", onehot, matrix, preferred_element_type=jnp.float32).astype(
        jnp.bfloat16
    )


def shards(
    exchange_integral_halves,
    amplitudes,
    pair_slot_orbitals,
    pao_domain,
    pao_intersection,
    pao_fock,
    occ_energy,
    coupled_pair_owner,
    coupled_pair_slot,
    coupling_swap_flag,
    coupling_fock_element,
):
    slot_count, extent = (amplitudes.shape[0], amplitudes.shape[1])
    paos = pao_intersection.shape[0]
    halves = lax.axis_size("aux")
    owner_index = lax.axis_index("orb")
    aux_index = lax.axis_index("aux")
    half_rows = extent // halves
    row_first = aux_index * half_rows
    every_amp = lax.all_gather(amplitudes, "orb", axis=0, tiled=True)
    own_slots = owner_index * slot_count + jnp.arange(slot_count, dtype=jnp.int32)
    orb_i = pair_slot_orbitals[own_slots, 0]
    orb_j = pair_slot_orbitals[own_slots, 1]
    dom_i = pao_domain[orb_i]
    dom_j = pao_domain[orb_j]
    rows_dom = lax.dynamic_slice_in_dim(dom_i, row_first, half_rows, 1)
    energy_sum = occ_energy[orb_i] + occ_energy[orb_j]
    global_slot = coupled_pair_owner * slot_count + coupled_pair_slot
    flipped = coupling_swap_flag == 1
    first_orb = pair_slot_orbitals[global_slot, 0]
    second_orb = pair_slot_orbitals[global_slot, 1]
    orb_p = jnp.where(flipped, second_orb, first_orb)
    orb_q = jnp.where(flipped, first_orb, second_orb)
    oh_rows = one_hot(rows_dom, paos)
    oh_i = one_hot(dom_i, paos)
    oh_j = one_hot(dom_j, paos)
    oh_p = one_hot(pao_domain[orb_p], paos)
    oh_q = one_hot(pao_domain[orb_q], paos)
    rs = sel_rows(oh_rows, pao_intersection)
    rf = sel_rows(oh_rows, pao_fock)
    s_ii = jnp.einsum("brk,bak->bra", rs, oh_i, preferred_element_type=jnp.float32).astype(
        jnp.bfloat16
    )
    f_ii = jnp.einsum("brk,bak->bra", rf, oh_i, preferred_element_type=jnp.float32).astype(
        jnp.bfloat16
    )
    js = sel_rows(oh_j, pao_intersection)
    jf = sel_rows(oh_j, pao_fock)
    s_jj = jnp.einsum("bjk,bak->bja", js, oh_j, preferred_element_type=jnp.float32).astype(
        jnp.bfloat16
    )
    f_jj = jnp.einsum("bjk,bak->bja", jf, oh_j, preferred_element_type=jnp.float32).astype(
        jnp.bfloat16
    )
    col_s = jnp.einsum(
        "kc,bjc->bkj", pao_intersection, oh_j, preferred_element_type=jnp.float32
    ).astype(jnp.bfloat16)
    s_ip = jnp.einsum("brk,bcpk->bcrp", rs, oh_p, preferred_element_type=jnp.float32).astype(
        jnp.bfloat16
    )
    s_qj = jnp.einsum("bcqk,bkj->bcqj", oh_q, col_s, preferred_element_type=jnp.float32).astype(
        jnp.bfloat16
    )
    summed = lax.psum_scatter(exchange_integral_halves[0], "aux", scatter_dimension=1, tiled=True)
    left_f = jnp.einsum(
        "bra,bad->brd", f_ii, amplitudes, preferred_element_type=jnp.float32
    ).astype(jnp.bfloat16)
    left_s = jnp.einsum(
        "bra,bad->brd", s_ii, amplitudes, preferred_element_type=jnp.float32
    ).astype(jnp.bfloat16)
    summed = summed + jnp.einsum("brd,bdj->brj", left_f, s_jj, preferred_element_type=jnp.float32)
    summed = summed + jnp.einsum("brd,bdj->brj", left_s, f_jj, preferred_element_type=jnp.float32)
    summed = summed - energy_sum[:, None, None] * jnp.einsum(
        "brd,bdj->brj", left_s, s_jj, preferred_element_type=jnp.float32
    )
    blocks = every_amp[global_slot]
    blocks = jnp.where(flipped[:, :, None, None], jnp.swapaxes(blocks, 2, 3), blocks)
    reach = jnp.einsum("bcrp,bcpd->bcrd", s_ip, blocks, preferred_element_type=jnp.float32).astype(
        jnp.bfloat16
    )
    for column in range(coupled_pair_owner.shape[1]):
        summed = summed - coupling_fock_element[:, column][:, None, None] * jnp.einsum(
            "brd,bdj->brj", reach[:, column], s_qj[:, column], preferred_element_type=jnp.float32
        )
    pao_energy = jnp.diagonal(pao_fock).astype(jnp.float32)
    denom = (
        pao_energy[rows_dom][:, :, None] + pao_energy[dom_j][:, None, :] - energy_sum[:, None, None]
    )
    amp_rows = lax.dynamic_slice_in_dim(amplitudes, row_first, half_rows, 1).astype(jnp.float32)
    updated = (amp_rows - summed / denom).astype(jnp.bfloat16)
    return (summed, updated)


def solution(mesh):
    placed = (
        P("aux", ("groups", "orb"), None, None),
        P(("groups", "orb"), None, None),
        P("groups", None),
        P("groups", None),
        P("groups", None),
        P("groups", None),
        P("groups"),
        P(("groups", "orb"), None),
        P(("groups", "orb"), None),
        P(("groups", "orb"), None),
        P(("groups", "orb"), None),
    )
    return jax.shard_map(
        shards,
        mesh=mesh,
        in_specs=placed,
        out_specs=(P(("groups", "orb"), "aux", None), P(("groups", "orb"), "aux", None)),
        check_vma=False,
    )
```

profile of v0, /device:TPU:0, one launch (start us, length us, event | category | flops | bytes accessed | tf_op | source)
XLA Modules:
  0.0 166.4 jit_solution(18155204422644652714)
XLA Ops:
  7.2 0.7 all-gather.2.cloned.1.call-update
  7.9 1.3 gather_fusion.2
  9.3 1.3 gather_fusion
  10.6 1.3 gather_fusion.4
  11.9 1.4 gather_fusion.1
  13.3 1.3 gather_fusion.5
  14.6 1.4 gather_fusion.3
  16.0 8.0 %gather_fusion.11 = bf16[512]{0:T(512)(128)(2,1)S(1)} fusion(bf16[512,512]{1,0:T(8,128)(2,1)} %param.16, s32[512]{0:T(512)S(1)} %bitcast.130), kind=kCustom, calls=%fused_computation.11 | custom fusion | bytes 6144 | tf_op jit(solution)/shard_map/jit(diagonal)/cond/branch_0_fun/gather | solution.py:102
  24.1 6.9 %gather_fusion.13 = f32[1024]{0:T(1024)S(1)} fusion(f32[512]{0:T(512)S(1)} %convert_element_type.73, s32[1024]{0:T(1024)S(1)} %broadcast_clamp_fusion), kind=kCustom, calls=%fused_computation.13 | custom fusion | bytes 12288 | tf_op jit(solution)/shard_map/gather | solution.py:104
  31.1 6.9 %gather_fusion.12 = f32[1024]{0:T(1024)S(1)} fusion(f32[512]{0:T(512)S(1)} %convert_element_type.73, s32[1024]{0:T(1024)S(1)} %broadcast_clamp_fusion.1), kind=kCustom, calls=%fused_computation.12 | custom fusion | bytes 12288 | tf_op jit(solution)/shard_map/gather | solution.py:104
  38.1 0.8 gather_fusion.6
  39.0 0.8 gather_fusion.7
  40.2 0.6 gather_fusion.10
  40.8 0.6 gather_fusion.8
  41.7 1.7 %fusion.28.clone.5 = bf16[4,256,512,1]{2,1,3,0:T(8,128)(2,1)} fusion(s32[4,256]{1,0:T(4,128)S(1)} %gather_fusion.3, bf16[512,512]{1,0:T(8,128)(2,1)S(1)} %copy-done), kind=kOutput, calls=%fused_computation.42.clone.clone.clone.2 | convolution fusion | flops 537919488 | bytes 1576960 | tf_op jit(solution)/shard_map/kc,bjc->bkj/dot_general | solution.py:72
  43.5 1.1 fusion.40
  44.6 1.9 %fusion.41 = bf16[4,256,256]{2,1,0:T(8,128)(2,1)} fusion(s32[4,256]{1,0:T(4,128)S(1)} %gather_fusion.3, bf16[512,512]{1,0:T(8,128)(2,1)S(1)} %copy-done.6), kind=kOutput, calls=%fused_computation.66 | convolution fusion | flops 807141376 | bytes 1052672 | tf_op jit(solution)/shard_map/bjk,bak->bja/dot_general | solution.py:69
  46.5 1.9 %fusion.38 = bf16[4,256,256]{2,1,0:T(8,128)(2,1)} fusion(s32[4,256]{1,0:T(4,128)S(1)} %gather_fusion.1, bf16[512,512]{1,0:T(8,128)(2,1)S(1)} %copy-done.6), kind=kOutput, calls=%fused_computation.63 | convolution fusion | flops 807141376 | bytes 1052672 | tf_op jit(solution)/shard_map/brk,bak->bra/dot_general | solution.py:61
  48.4 1.7 %fusion.24 = bf16[4,256,512]{2,1,0:T(8,128)(2,1)} fusion(s32[4,256]{1,0:T(4,128)S(1)} %gather_fusion.1, bf16[512,512]{1,0:T(8,128)(2,1)S(1)} %copy-done), kind=kOutput, calls=%fused_computation.38 | convolution fusion | flops 537919488 | bytes 1576960 | tf_op jit(solution)/shard_map/...rk,kc->...rc/dot_general | solution.py:12
  50.2 2.0 %convolution_convert_fusion = bf16[4,256,256]{2,1,0:T(8,128)(2,1)S(1)} fusion(bf16[4,256,256]{2,1,0:T(8,128)(2,1)S(1)} %copy-done.5, bf16[4,256,512]{2,1,0:T(8,128)(2,1)} %fusion.24, s32[4,256]{1,0:T(4,128)S(1)} %gather_fusion.1), kind=kOutput, calls=%fused_computation.67 | convolution fusion | flops 403701760 | bytes 2101248 | tf_op jit(solution)/shard_map/bra,bad->brd/dot_general | solution.py:85
  52.2 1.8 %convolution_add_fusion.1 = f32[4,256,256]{2,1,0:T(8,128)S(1)} fusion(bf16[4,256,256]{2,1,0:T(8,128)(2,1)S(1)} %fusion.40, bf16[4,256,256]{2,1,0:T(8,128)(2,1)} %fusion.38, bf16[4,256,256]{2,1,0:T(8,128)(2,1)S(1)} %copy-done.5, f32[1,4,256,256]{3,2,1,0:T(8,128)} %param.11), kind=kOutput, calls=%fused_computation.62 | convolution fusion | flops 268959744 | bytes 3670016 | tf_op jit(solution)/shard_map/brd,bdj->brj/dot_general | solution.py:88
  54.1 1.4 convolution_add_fusion
  55.8 4.6 %fusion.13 = bf16[4,8,256,256]{3,2,1,0:T(8,128)(2,1)} fusion(s32[4,8,256]{2,1,0:T(8,128)S(1)} %bitcast.134, bf16[4,256,512,1]{2,1,3,0:T(8,128)(2,1)S(1)} %copy-done.12), kind=kOutput, calls=%fused_computation.25 | convolution fusion | flops 2153775104 | bytes 5275648 | tf_op jit(solution)/shard_map/bcqk,bkj->bcqj/dot_general | solution.py:78
  60.4 68.1 %all-gather.2.cloned.1.call-done = bf16[128,256,256]{2,1,0:T(8,128)(2,1)} async-done(((bf16[4,256,256]{2,1,0:T(8,128)(2,1)}), bf16[128,256,256]{2,1,0:T(8,128)(2,1)}) %all-gather.2.cloned.1.call-update) | async-done | bytes 16777232 | tf_op jit(solution)/shard_map/all_gather | solution.py:37
  128.5 8.6 %gather_fusion.9 = bf16[32,256,256]{2,1,0:T(8,128)(2,1)} fusion(bf16[128,256,256]{2,1,0:T(8,128)(2,1)} %all-gather.2.cloned.1.call-done, s32[1024]{0:T(1024)S(1)} %pad_clamp_fusion.1), kind=kCustom, calls=%fused_computation.9 | custom fusion | bytes 8388736 | tf_op jit(solution)/shard_map/gather | solution.py:93
  137.0 6.3 %copy.15 = bf16[4,8,256,256]{3,2,1,0:T(8,128)(2,1)} copy(bf16[4,8,256,256]{2,3,1,0:T(8,128)(2,1)} %bitcast.131) | data formatting | bytes 8388608 | tf_op jit(solution)/shard_map/transpose | solution.py:94
  143.3 8.1 %fusion.8 = bf16[4,8,256,256]{3,2,1,0:T(8,128)(2,1)} fusion(bf16[4,8,256,256]{3,2,1,0:T(8,128)(2,1)} %copy.15, bf16[4,8,256,256]{3,2,1,0:T(8,128)(2,1)} %bitcast.132, pred[4,8]{1,0:T(4,128)(4,1)S(1)} %get-tuple-element.11, s32[4,8,256]{2,1,0:T(8,128)S(1)} %bitcast.133, bf16[4,256,512]{2,1,0:T(8,128)(2,1)S(1)} %copy-done.11), kind=kOutput, calls=%fused_computation.24 | convolution fusion | flops 3231711232 | bytes 13664288 | tf_op jit(solution)/shard_map/bcrp,bcpd->bcrd/dot_general | solution.py:95
  151.4 1.7 fusion.36
  153.1 2.3 %fusion.35 = f32[4,256,256]{2,1,0:T(8,128)S(1)} fusion(f32[4,256,256]{2,1,0:T(8,128)S(1)} %fusion.36, bf16[4,8,256,256]{3,2,1,0:T(8,128)(2,1)} %fusion.13, bf16[4,8,256,256]{3,2,1,0:T(8,128)(2,1)} %fusion.8, f32[4]{0:T(128)S(1)} %get-tuple-element.7), kind=kOutput, calls=%fused_computation.56 | convolution fusion | flops 134742016 | bytes 3145744 | tf_op jit(solution)/shard_map/brd,bdj->brj/dot_general | solution.py:99
  155.3 1.4 fusion.34
  156.7 0.3 fusion.33
  158.0 1.6 subtract_convert_fusion
  (62 shorter events, 2.3 us)
Async XLA Ops:
  7.2 34.6 %copy-start = (bf16[512,512]{1,0:T(8,128)(2,1)S(1)}, bf16[512,512]{1,0:T(8,128)(2,1)}, u32[]{:S(2)}) copy-start(bf16[512,512]{1,0:T(8,128)(2,1)} %param.15) | copy-start | bytes 1572868
  7.2 121.3 %all-gather.2.cloned.1.call-start = ((), (), s32[]{:S(2)}) async-start(), calls=%async_computation | async-start | bytes 17301504 | tf_op jit(solution)/shard_map/all_gather | solution.py:37
  24.1 13.9 %copy-start.9 = (s32[4,8]{1,0:T(4,128)S(1)}, s32[4,8]{1,0:T(4,128)}, u32[]{:S(2)}) copy-start(s32[4,8]{1,0:T(4,128)} %param.19) | copy-start | bytes 388
  24.1 13.9 %copy-start.10 = (s32[4,8]{1,0:T(4,128)S(1)}, s32[4,8]{1,0:T(4,128)}, u32[]{:S(2)}) copy-start(s32[4,8]{1,0:T(4,128)} %param.18) | copy-start | bytes 388
  24.1 14.0 %copy-start.1 = (s32[128,2]{0,1:T(2,128)S(1)}, s32[128,2]{0,1:T(2,128)}, u32[]{:S(2)}) copy-start(s32[128,2]{0,1:T(2,128)} %param.13) | copy-start | bytes 3076
  31.1 8.9 %copy-start.8 = (s32[4,8]{1,0:T(4,128)S(1)}, s32[4,8]{1,0:T(4,128)}, u32[]{:S(2)}) copy-start(s32[4,8]{1,0:T(4,128)} %param.20) | copy-start | bytes 388
  31.1 9.1 %copy-start.2 = (s32[64,256]{1,0:T(8,128)S(1)}, s32[64,256]{1,0:T(8,128)}, u32[]{:S(2)}) copy-start(s32[64,256]{1,0:T(8,128)} %param.14) | copy-start | bytes 196612
  31.1 10.3 %copy-start.7 = (f32[4,8]{1,0:T(4,128)S(1)}, f32[4,8]{1,0:T(4,128)}, u32[]{:S(2)}) copy-start(f32[4,8]{1,0:T(4,128)} %param.21) | copy-start | bytes 388
  39.8 4.8 %copy-start.6 = (bf16[512,512]{1,0:T(8,128)(2,1)S(1)}, bf16[512,512]{1,0:T(8,128)(2,1)}, u32[]{:S(2)}) copy-start(bf16[512,512]{1,0:T(8,128)(2,1)} %param.16) | copy-start | bytes 1572868
  46.5 3.6 %copy-start.5 = (bf16[4,256,256]{2,1,0:T(8,128)(2,1)S(1)}, bf16[4,256,256]{2,1,0:T(8,128)(2,1)}, u32[]{:S(2)}) copy-start(bf16[4,256,256]{2,1,0:T(8,128)(2,1)} %param.12) | copy-start | bytes 1572868
  54.0 1.8 %copy-start.12 = (bf16[4,256,512,1]{2,1,3,0:T(8,128)(2,1)S(1)}, bf16[4,256,512,1]{2,1,3,0:T(8,128)(2,1)}, u32[]{:S(2)}) copy-start(bf16[4,256,512,1]{2,1,3,0:T(8,128)(2,1)} %fusion.28.clone.5) | copy-start | bytes 3145732
  137.0 6.3 %copy-start.11 = (bf16[4,256,512]{2,1,0:T(8,128)(2,1)S(1)}, bf16[4,256,512]{2,1,0:T(8,128)(2,1)}, u32[]{:S(2)}) copy-start(bf16[4,256,512]{2,1,0:T(8,128)(2,1)} %fusion.24) | copy-start | bytes 3145732
  151.4 3.9 %copy-start.3 = (bf16[4,8,256,256]{3,2,1,0:T(8,128)(2,1)S(1)}, bf16[4,8,256,256]{3,2,1,0:T(8,128)(2,1)}, u32[]{:S(2)}) copy-start(bf16[4,8,256,256]{3,2,1,0:T(8,128)(2,1)} %fusion.13) | copy-start | bytes 12582916
  151.4 5.3 %copy-start.4 = (bf16[4,8,256,256]{3,2,1,0:T(8,128)(2,1)S(1)}, bf16[4,8,256,256]{3,2,1,0:T(8,128)(2,1)}, u32[]{:S(2)}) copy-start(bf16[4,8,256,256]{3,2,1,0:T(8,128)(2,1)} %fusion.8) | copy-start | bytes 12582916
Sparse Core Ops, SparseCore 0:
  10.9 117.5 all-gather.1
where the time goes:
time: 167 us; the launch traced here: 166 us
  waiting for transfers between devices  68.8 us (41%)
  local copies, waits for them, and re-layouts  48.3 us (29%)
  matrix products  34.8 us (21%)
  between operations  14.4 us (9%)
    all_gather x1, waiting for transfers between devices, shards(): every_amp = lax.all_gather(amplitudes, 'orb', axis=0, tiled=True)  68.1 us
    gather x1, local copies, waits for them, and re-layouts, shards(): blocks = every_amp[global_slot]  8.55 us
    dot_general x8, matrix products, shards(): jnp.einsum('brd,bdj->brj', reach[:, column], s_qj[:, column], preferred_e...  8.1 us
    dot_general x1, matrix products, shards(): jnp.einsum('bcrp,bcpd->bcrd', s_ip, blocks, preferred_element_type=jnp.fl...  8.09 us
    gather x1, local copies, waits for them, and re-layouts, shards(): pao_energy = jnp.diagonal(pao_fock).astype(jnp.float32)  8.03 us
    gather x2, local copies, waits for them, and re-layouts, shards(): pao_energy[dom_j][:, None, :]  6.88 us
    gather x2, local copies, waits for them, and re-layouts, shards(): pao_energy[rows_dom][:, :, None] + pao_energy[dom_j][:, None, :]  6.88 us
    transpose x1, local copies, waits for them, and re-layouts, shards(): jnp.swapaxes(blocks, 2, 3)  6.29 us
  transfers between devices with their start and end apart: 1, of which 1 were waited for; matrix products, arithmetic and copies ran while one was open for 31% of the time, Pallas kernels for 0%

commit v1 on v0

--- a/solution.py
+++ b/solution.py
@@ -34,7 +34,17 @@
     aux_index = lax.axis_index("aux")
     half_rows = extent // halves
     row_first = aux_index * half_rows
-    every_amp = lax.all_gather(amplitudes, "orb", axis=0, tiled=True)
+    newest = lax.axis_size("orb")
+    outer = lax.axis_index("orb")
+    latest, tile_out = (newest, outer)
+    every_amp, now = (amplitudes, 1)
+    while now < latest:
+        x_next = tuple(((dev_j, dev_j ^ now) for dev_j in range(latest)))
+        t1 = lax.ppermute(every_amp, "orb", x_next)
+        mixed_arr = jnp.concatenate([every_amp, t1], 0)
+        m_next = jnp.concatenate([t1, every_amp], 0)
+        every_amp = jnp.where(tile_out & now == 0, mixed_arr, m_next)
+        now = 2 * now
     own_slots = owner_index * slot_count + jnp.arange(slot_count, dtype=jnp.int32)
     orb_i = pair_slot_orbitals[own_slots, 0]
     orb_j = pair_slot_orbitals[own_slots, 1]

time: 167 us -> 596 us (3.57)
  waiting for transfers between devices: 68.8 us -> 476 us
  other arithmetic: 0.11 us -> 35.1 us
  between operations: 14.4 us -> 1.03 us
  starting transfers between devices: 0.04 us -> 9.02 us
  local copies, waits for them, and re-layouts: 48.3 us -> 40.8 us
    ppermute x0 -> x5, waiting for transfers between devices: none -> 476 us  [shards(): t1 = lax.ppermute(every_amp, 'orb', x_next)]
    all_gather x1 -> x0, waiting for transfers between devices: 68.1 us -> none  [shards(): every_amp = lax.all_gather(amplitudes, 'orb', axis=0, tiled=True)]
    select_n x0 -> x5, other arithmetic: none -> 34.9 us  [shards(): every_amp = jnp.where(tile_out & now == 0, mixed_arr, m_next)]
    ppermute x0 -> x5, starting transfers between devices: none -> 9.02 us  [shards(): t1 = lax.ppermute(every_amp, 'orb', x_next)]
  transfers between devices with their start and end apart: 1 -> 5, of which waited for: 1 -> 5; matrix products, arithmetic and copies ran while one was open for 31% -> 7% of each run, Pallas kernels for 0% -> 0%
where the time goes in v1:
time: 596 us
  waiting for transfers between devices  476 us (80%)
  local copies, waits for them, and re-layouts  40.8 us (7%)
  other arithmetic  35.1 us (6%)
  matrix products  34.3 us (6%)
  starting transfers between devices  9.02 us (2%)
    ppermute x5, waiting for transfers between devices, shards(): t1 = lax.ppermute(every_amp, 'orb', x_next)  476 us
    select_n x5, other arithmetic, shards(): every_amp = jnp.where(tile_out & now == 0, mixed_arr, m_next)  34.9 us
  transfers between devices with their start and end apart: 5, of which 5 were waited for; matrix products, arithmetic and copies ran while one was open for 7% of the time, Pallas kernels for 0%

profile of v1, /device:TPU:0, one launch (start us, length us, event | category | flops | bytes accessed | tf_op | source)
XLA Modules:
  0.0 596.0 jit_solution(4998061952478820700)
XLA Ops:
  1.2 1.7 collective-permute-done
  2.9 1.4 maximum_select_fusion.4
  4.3 2.9 collective-permute-start.1
  7.3 23.6 %collective-permute-done.1 = bf16[8,256,256]{2,1,0:T(8,128)(2,1)} collective-permute-done((bf16[8,256,256]{2,1,0:T(8,128)(2,1)S(1)}, bf16[8,256,256]{2,1,0:T(8,128)(2,1)}, u32[]{:S(2)}, u32[]{:S(2)}) %collective-permute-start.1) | collective-permute-done | bytes 1048608 | tf_op jit(solution)/shard_map/ppermute | solution.py:43
  30.8 2.8 maximum_select_fusion.3
  33.6 1.8 collective-permute-start.2
  35.5 45.5 %collective-permute-done.2 = bf16[16,256,256]{2,1,0:T(8,128)(2,1)} collective-permute-done((bf16[16,256,256]{2,1,0:T(8,128)(2,1)S(1)}, bf16[16,256,256]{2,1,0:T(8,128)(2,1)}, u32[]{:S(2)}, u32[]{:S(2)}) %collective-permute-start.2) | collective-permute-done | bytes 2097184 | tf_op jit(solution)/shard_map/ppermute | solution.py:43
  81.0 3.9 maximum_select_fusion.2
  84.8 1.5 collective-permute-start.3
  86.4 90.0 %collective-permute-done.3 = bf16[32,256,256]{2,1,0:T(8,128)(2,1)} collective-permute-done((bf16[32,256,256]{2,1,0:T(8,128)(2,1)}, bf16[32,256,256]{2,1,0:T(8,128)(2,1)}, u32[]{:S(2)}, u32[]{:S(2)}) %collective-permute-start.3) | collective-permute-done | bytes 4194336 | tf_op jit(solution)/shard_map/ppermute | solution.py:43
  176.4 9.3 %maximum_select_fusion.1 = bf16[64,256,256]{2,1,0:T(8,128)(2,1)} fusion(bf16[32,256,256]{2,1,0:T(8,128)(2,1)} %collective-permute-done.3, bf16[32,256,256]{2,1,0:T(8,128)(2,1)} %maximum_select_fusion.2, pred[]{:T(512)S(6)} %eq.92), kind=kLoop, calls=%fused_computation.19 | loop fusion | flops 12582912 | bytes 16777216 | tf_op jit(solution)/shard_map/jit(_where)/select_n | solution.py:46
  185.6 2.2 collective-permute-start.4
  195.1 4.8 gather_fusion.11
  200.0 6.9 %gather_fusion.12 = f32[1024]{0:T(1024)S(1)} fusion(f32[512]{0:T(512)S(1)} %convert_element_type.73, s32[1024]{0:T(1024)S(1)} %broadcast_clamp_fusion.1), kind=kCustom, calls=%fused_computation.12 | custom fusion | bytes 12288 | tf_op jit(solution)/shard_map/gather | solution.py:114
  206.9 6.9 %gather_fusion.13 = f32[1024]{0:T(1024)S(1)} fusion(f32[512]{0:T(512)S(1)} %convert_element_type.73, s32[1024]{0:T(1024)S(1)} %broadcast_clamp_fusion), kind=kCustom, calls=%fused_computation.13 | custom fusion | bytes 12288 | tf_op jit(solution)/shard_map/gather | solution.py:114
  214.1 1.7 fusion.28.clone.5
  217.0 1.1 fusion.38
  218.1 1.9 fusion.41
  220.0 1.7 fusion.24
  221.7 2.0 convolution_convert_fusion
  223.8 1.7 convolution_add_fusion.1
  225.4 1.4 convolution_add_fusion
  227.2 4.6 fusion.13
  231.8 315.1 %collective-permute-done.4 = bf16[64,256,256]{2,1,0:T(8,128)(2,1)} collective-permute-done((bf16[64,256,256]{2,1,0:T(8,128)(2,1)}, bf16[64,256,256]{2,1,0:T(8,128)(2,1)}, u32[]{:S(2)}, u32[]{:S(2)}) %collective-permute-start.4) | collective-permute-done | bytes 8388640 | tf_op jit(solution)/shard_map/ppermute | solution.py:43
  546.8 17.6 %maximum_select_fusion = bf16[128,256,256]{2,1,0:T(8,128)(2,1)} fusion(bf16[64,256,256]{2,1,0:T(8,128)(2,1)} %collective-permute-done.4, bf16[64,256,256]{2,1,0:T(8,128)(2,1)} %maximum_select_fusion.1, pred[]{:T(512)S(6)} %eq.91), kind=kLoop, calls=%fused_computation.14 | loop fusion | flops 25165824 | bytes 33554432 | tf_op jit(solution)/shard_map/jit(_where)/select_n | solution.py:46
  564.4 8.5 %gather_fusion.9 = bf16[32,256,256]{2,1,0:T(8,128)(2,1)} fusion(bf16[128,256,256]{2,1,0:T(8,128)(2,1)} %maximum_select_fusion, s32[1024]{0:T(1024)S(1)} %pad_clamp_fusion.1), kind=kCustom, calls=%fused_computation.9 | custom fusion | bytes 8388736 | tf_op jit(solution)/shard_map/gather | solution.py:103
  573.0 6.3 %copy.14 = bf16[4,8,256,256]{3,2,1,0:T(8,128)(2,1)} copy(bf16[4,8,256,256]{2,3,1,0:T(8,128)(2,1)} %bitcast.131) | data formatting | bytes 8388608 | tf_op jit(solution)/shard_map/transpose | solution.py:104
  579.3 8.6 %fusion.8 = bf16[4,8,256,256]{3,2,1,0:T(8,128)(2,1)} fusion(bf16[4,8,256,256]{3,2,1,0:T(8,128)(2,1)} %copy.14, bf16[4,8,256,256]{3,2,1,0:T(8,128)(2,1)} %bitcast.132, pred[4,8]{1,0:T(4,128)(4,1)S(1)} %get-tuple-element.11, s32[4,8,256]{2,1,0:T(8,128)S(1)} %bitcast.133, bf16[4,256,512]{2,1,0:T(8,128)(2,1)S(1)} %copy-done.14), kind=kOutput, calls=%fused_computation.27 | convolution fusion | flops 3231711232 | bytes 13664288 | tf_op jit(solution)/shard_map/bcrp,bcpd->bcrd/dot_general | solution.py:105
  587.9 1.7 fusion.36
  589.5 2.3 fusion.35
  591.8 1.4 fusion.34
  594.4 1.6 subtract_convert_fusion
  (80 shorter events, 10.7 us)
Async XLA Ops:
  0.6 213.5 %copy-start = (bf16[512,512]{1,0:T(8,128)(2,1)S(1)}, bf16[512,512]{1,0:T(8,128)(2,1)}, u32[]{:S(2)}) copy-start(bf16[512,512]{1,0:T(8,128)(2,1)} %param.15) | copy-start | bytes 1572868
  0.6 2.3 collective-permute-start
  4.3 2.9 copy-start.5
  4.3 26.5 %collective-permute-start.1 = (bf16[8,256,256]{2,1,0:T(8,128)(2,1)S(1)}, bf16[8,256,256]{2,1,0:T(8,128)(2,1)}, u32[]{:S(2)}, u32[]{:S(2)}) collective-permute-start(bf16[8,256,256]{2,1,0:T(8,128)(2,1)S(1)} %maximum_select_fusion.4), channel_id=1, source_target_pairs={{0,2},{1,3},{2,0},{3,1},{4,6},{5,7},{6,4},{7,5},{8,10},{9,11},{10,... | collective-permute-start | bytes 3145736 | tf_op jit(solution)/shard_map/ppermute | solution.py:43
  33.6 47.3 %collective-permute-start.2 = (bf16[16,256,256]{2,1,0:T(8,128)(2,1)S(1)}, bf16[16,256,256]{2,1,0:T(8,128)(2,1)}, u32[]{:S(2)}, u32[]{:S(2)}) collective-permute-start(bf16[16,256,256]{2,1,0:T(8,128)(2,1)S(1)} %maximum_select_fusion.3), channel_id=1, source_target_pairs={{0,4},{1,5},{2,6},{3,7},{4,0},{5,1},{6,2},{7,3},{8,12},{9,13},{10,... | collective-permute-start | bytes 6291464 | tf_op jit(solution)/shard_map/ppermute | solution.py:43
  84.8 91.5 %collective-permute-start.3 = (bf16[32,256,256]{2,1,0:T(8,128)(2,1)}, bf16[32,256,256]{2,1,0:T(8,128)(2,1)}, u32[]{:S(2)}, u32[]{:S(2)}) collective-permute-start(bf16[32,256,256]{2,1,0:T(8,128)(2,1)} %maximum_select_fusion.2), channel_id=1, source_target_pairs={{0,8},{1,9},{2,10},{3,11},{4,12},{5,13},{6,14},{7,15},{8,0},{9,1},... | collective-permute-start | bytes 12582920 | tf_op jit(solution)/shard_map/ppermute | solution.py:43
  86.4 101.5 %copy-start.2 = (s32[128,2]{0,1:T(2,128)S(1)}, s32[128,2]{0,1:T(2,128)}, u32[]{:S(2)}) copy-start(s32[128,2]{0,1:T(2,128)} %param.13) | copy-start | bytes 3076
  86.4 102.8 %copy-start.4 = (s32[64,256]{1,0:T(8,128)S(1)}, s32[64,256]{1,0:T(8,128)}, u32[]{:S(2)}) copy-start(s32[64,256]{1,0:T(8,128)} %param.14) | copy-start | bytes 196612
  86.4 104.0 %copy-start.3 = (f32[64]{0:T(128)S(1)}, f32[64]{0:T(128)}, u32[]{:S(2)}) copy-start(f32[64]{0:T(128)} %param.17) | copy-start | bytes 772
  86.4 105.3 %copy-start.12 = (s32[4,8]{1,0:T(4,128)S(1)}, s32[4,8]{1,0:T(4,128)}, u32[]{:S(2)}) copy-start(s32[4,8]{1,0:T(4,128)} %param.19) | copy-start | bytes 388
  86.4 105.3 %copy-start.13 = (s32[4,8]{1,0:T(4,128)S(1)}, s32[4,8]{1,0:T(4,128)}, u32[]{:S(2)}) copy-start(s32[4,8]{1,0:T(4,128)} %param.18) | copy-start | bytes 388
  185.6 8.0 %copy-start.11 = (s32[4,8]{1,0:T(4,128)S(1)}, s32[4,8]{1,0:T(4,128)}, u32[]{:S(2)}) copy-start(s32[4,8]{1,0:T(4,128)} %param.20) | copy-start | bytes 388
  185.6 9.4 %copy-start.9 = (bf16[512,512]{1,0:T(8,128)(2,1)S(1)}, bf16[512,512]{1,0:T(8,128)(2,1)}, u32[]{:S(2)}) copy-start(bf16[512,512]{1,0:T(8,128)(2,1)} %param.16) | copy-start | bytes 1572868
  185.6 361.2 %collective-permute-start.4 = (bf16[64,256,256]{2,1,0:T(8,128)(2,1)}, bf16[64,256,256]{2,1,0:T(8,128)(2,1)}, u32[]{:S(2)}, u32[]{:S(2)}) collective-permute-start(bf16[64,256,256]{2,1,0:T(8,128)(2,1)} %maximum_select_fusion.1), channel_id=1, source_target_pairs={{0,16},{1,17},{2,18},{3,19},{4,20},{5,21},{6,22},{7,23},{8,24},{9,... | collective-permute-start | bytes 25165832 | tf_op jit(solution)/shard_map/ppermute | solution.py:43
  199.9 13.8 %copy-start.10 = (f32[4,8]{1,0:T(4,128)S(1)}, f32[4,8]{1,0:T(4,128)}, u32[]{:S(2)}) copy-start(f32[4,8]{1,0:T(4,128)} %param.21) | copy-start | bytes 388
  218.1 3.7 copy-start.8
  225.4 1.8 copy-start.15
  573.0 6.3 %copy-start.14 = (bf16[4,256,512]{2,1,0:T(8,128)(2,1)S(1)}, bf16[4,256,512]{2,1,0:T(8,128)(2,1)}, u32[]{:S(2)}) copy-start(bf16[4,256,512]{2,1,0:T(8,128)(2,1)} %fusion.24) | copy-start | bytes 3145732
  587.8 3.9 copy-start.6
  587.9 5.3 copy-start.7
  594.1 1.9 copy-start.1
